TPU v7x, 32 devices: a whole 2x2x4 slice. The times are simulated.
32 devices in a mesh: replica: 4 (over y, core), fsdp: 2 (over x), tensor: 4 (over z).
Axes of the slice: x: 2, y: 2, z: 4, core: 2. Of those that a mesh axis runs over, the one named last changes fastest.
Arguments:
- grad_parts: bfloat16 [4, 2, 512, 8192], P('replica', 'fsdp', 'tensor'), may hold values from -12 to 12
- inner_params: float32 [4, 512, 8192], P('replica', 'tensor', 'fsdp'), may hold values from -0.12 to 0.12
- first_moment: float32 [4, 512, 8192], P('replica', 'tensor', 'fsdp'), may hold values from -4 to 4
- second_moment: float32 [4, 512, 8192], P('replica', 'tensor', 'fsdp'), may hold values from 0.1 to 10
- outer_params: float32 [4, 512, 2048], P('replica', 'tensor', 'fsdp'), may hold values from -0.12 to 0.12
- outer_momentum: float32 [4, 512, 2048], P('replica', 'tensor', 'fsdp'), may hold values from -0.06 to 0.06
Outputs:
- next_weights: float32 [512, 8192], P('tensor')
- outer_params_out: float32 [4, 512, 2048], P('replica', 'tensor', 'fsdp')
- outer_momentum_out: float32 [4, 512, 2048], P('replica', 'tensor', 'fsdp')
- first_out: float32 [4, 512, 8192], P('replica', 'tensor', 'fsdp')
- second_out: float32 [4, 512, 8192], P('replica', 'tensor', 'fsdp')
All inputs are finite; a program needn't handle non-finite values.
Results may differ from a plain program's by a relative error of at most 0.0003.
Values may be sent and summed in bfloat16 or wider, within the bound.
No kernel may reach another device: no remote copies, remote signals or barrier semaphores. Data moves between devices by JAX's collectives and lax.ppermute only.
A program may use at most 64 MiB of HBM per device.

v0:
```python
import jax
import jax.numpy as jnp
from jax import lax
from jax.sharding import PartitionSpec as P

STEP = 100
beta_first = 0.9
beta_second = 0.95
inner_rate = 0.01
weight_decay = 0.1
epsilon = 1e-08
outer_rate = 0.7
momentum_factor = 0.9


def inner_adamw(gradient, params, first_in, second_in):
    first_out = beta_first * first_in + (1.0 - beta_first) * gradient
    second_out = beta_second * second_in + (1.0 - beta_second) * gradient * gradient
    first_scale = 1.0 / (1.0 - beta_first**STEP)
    second_scale = 1.0 / (1.0 - beta_second**STEP)
    direction = first_out * first_scale / (jnp.sqrt(second_out * second_scale) + epsilon)
    updated = params - inner_rate * (direction + weight_decay * params)
    return (first_out, second_out, updated)


def nesterov(mean_params, outer_in, momentum):
    pseudo_grad = outer_in - mean_params
    momentum_new = momentum_factor * momentum + pseudo_grad
    params_new = outer_in - outer_rate * (pseudo_grad + momentum_factor * momentum_new)
    return (params_new, momentum_new)


def local(grad_parts, inner_params, first_moment, second_moment, outer_params, outer_momentum):
    replicas = lax.axis_size("replica")
    gradient = lax.psum_scatter(
        grad_parts[0, 0].astype(jnp.float32), "fsdp", scatter_dimension=1, tiled=True
    )
    first_out, second_out, updated = inner_adamw(
        gradient, inner_params[0], first_moment[0], second_moment[0]
    )
    share_cols = outer_params.shape[2]
    totals = lax.psum_scatter(updated, "replica", scatter_dimension=1, tiled=True)
    params_new, momentum_new = nesterov(totals / replicas, outer_params[0], outer_momentum[0])
    pieces = lax.all_gather(params_new[None], ("replica", "fsdp"), axis=0, tiled=True)
    fsdp_count = lax.axis_size("fsdp")
    row_count = params_new.shape[0]
    arranged = pieces.reshape(replicas, fsdp_count, row_count, share_cols).transpose(2, 1, 0, 3)
    next_weights = arranged.reshape(row_count, fsdp_count * replicas * share_cols)
    return (next_weights, params_new[None], momentum_new[None], first_out[None], second_out[None])


def solution(mesh):
    return jax.shard_map(
        local,
        mesh=mesh,
        in_specs=(
            P("replica", "fsdp", "tensor", None),
            P("replica", "tensor", "fsdp"),
            P("replica", "tensor", "fsdp"),
            P("replica", "tensor", "fsdp"),
            P("replica", "tensor", "fsdp"),
            P("replica", "tensor", "fsdp"),
        ),
        out_specs=(
            P("tensor", None),
            P("replica", "tensor", "fsdp"),
            P("replica", "tensor", "fsdp"),
            P("replica", "tensor", "fsdp"),
            P("replica", "tensor", "fsdp"),
        ),
        check_vma=False,
    )
```

profile of v0, /device:TPU:0, one launch (start us, length us, event | category | flops | bytes accessed | tf_op | source)
XLA Modules:
  0.0 165.5 jit_solution(11605220158875495596)
XLA Ops:
  7.2 0.0 reduce-scatter.3.cloned.1.call-start
  7.2 4.0 %bitcast_convert_fusion = f32[128,8192]{1,0:T(8,128)} fusion(bf16[1,1,128,8192]{3,2,1,0:T(8,128)(2,1)} %param.6), kind=kLoop, calls=%fused_computation.2 | loop fusion | flops 1048576 | bytes 6291456 | tf_op jit(solution)/shard_map/convert_element_type | solution.py:36
  11.2 0.0 copy-start
  11.2 0.0 reduce-scatter.3.cloned.1.call-update
  11.3 0.0 reduce-scatter.5.cloned.1.call-start
  11.3 57.2 %reduce-scatter.3.cloned.1.call-done = f32[128,4096]{1,0:T(8,128)} async-done(((f32[128,8192]{1,0:T(8,128)}), f32[128,4096]{1,0:T(8,128)}) %reduce-scatter.3.cloned.1.call-update) | async-done | bytes 2097168 | tf_op jit(solution)/shard_map/reduce_scatter | solution.py:35
  68.5 0.0 copy-done
  68.5 7.1 %fusion.4 = (f32[1,128,4096]{2,1,0:T(8,128)}, f32[128,4096]{1,0:T(8,128)}, f32[1,128,4096]{2,1,0:T(8,128)}) fusion(f32[128,4096]{1,0:T(8,128)} %reduce-scatter.3.cloned.1.call-done, f32[1,128,4096]{2,1,0:T(8,128)S(1)} %copy-done, f32[1,128,4096]{2,1,0:T(8,128)} %param.8, f32[1,128,4096]{2,1,0:T(8,128)} %param.7), kind=kLoop, calls=%fused_computation.9 | loop fusion | flops 7864320 | bytes 14680064 | tf_op jit(solution)/shard_map/broadcast_in_dim | solution.py:49
  75.6 0.0 copy-start.1
  75.7 0.0 copy-start.2
  75.7 0.0 reduce-scatter.5.cloned.1.call-update
  75.7 0.0 all-gather.3.cloned.1.call-start
  75.7 31.3 %reduce-scatter.5.cloned.1.call-done = f32[128,1024]{1,0:T(8,128)} async-done(((f32[128,4096]{1,0:T(8,128)}), f32[128,1024]{1,0:T(8,128)}) %reduce-scatter.5.cloned.1.call-update) | async-done | bytes 524304 | tf_op jit(solution)/shard_map/reduce_scatter | solution.py:42
  107.0 0.0 copy-done.1
  107.0 0.0 copy-done.2
  107.0 2.2 %fusion.5 = (f32[1,128,1024]{2,1,0:T(8,128)}, f32[128,1024]{1,0:T(8,128)}) fusion(f32[128,1024]{1,0:T(8,128)} %reduce-scatter.5.cloned.1.call-done, f32[1,128,1024]{2,1,0:T(8,128)S(1)} %copy-done.1, f32[1,128,1024]{2,1,0:T(8,128)S(1)} %copy-done.2), kind=kLoop, calls=%fused_computation.13 | loop fusion | flops 1048576 | bytes 2621440 | tf_op jit(solution)/shard_map/broadcast_in_dim | solution.py:49
  109.2 0.0 all-gather.3.cloned.1.call-update
  109.2 36.9 %all-gather.3.cloned.1.call-done = f32[1024,1024]{1,0:T(8,128)} async-done(((f32[128,1024]{1,0:T(8,128)}), f32[1024,1024]{1,0:T(8,128)}) %all-gather.3.cloned.1.call-update) | async-done | bytes 4194320 | tf_op jit(solution)/shard_map/all_gather | solution.py:44
  146.1 6.9 %copy.11 = f32[128,2,4,1024]{3,2,1,0:T(4,128)} copy(f32[128,2,4,1024]{3,0,1,2:T(8,128)} %bitcast.51) | data formatting | bytes 8388608 | tf_op jit(solution)/shard_map/transpose | solution.py:47
  153.0 6.0 %reshape.25 = f32[128,8192]{1,0:T(8,128)} reshape(f32[128,2,4,1024]{3,2,1,0:T(4,128)} %copy.11) | data formatting | bytes 8388608 | tf_op jit(solution)/shard_map/reshape | solution.py:48
Async XLA Ops:
  7.2 61.4 %reduce-scatter.3.cloned.1.call-start = ((), (), s32[]{:S(2)}) async-start(), calls=%async_computation.2 | async-start | bytes 6291456 | tf_op jit(solution)/shard_map/reduce_scatter | solution.py:35
  11.2 57.3 %copy-start = (f32[1,128,4096]{2,1,0:T(8,128)S(1)}, f32[1,128,4096]{2,1,0:T(8,128)}, u32[]{:S(2)}) copy-start(f32[1,128,4096]{2,1,0:T(8,128)} %param.9) | copy-start | bytes 6291460
  11.3 95.8 %reduce-scatter.5.cloned.1.call-start = ((), (), s32[]{:S(2)}) async-start(), calls=%async_computation.3 | async-start | bytes 2621440 | tf_op jit(solution)/shard_map/reduce_scatter | solution.py:42
  75.6 31.4 %copy-start.1 = (f32[1,128,1024]{2,1,0:T(8,128)S(1)}, f32[1,128,1024]{2,1,0:T(8,128)}, u32[]{:S(2)}) copy-start(f32[1,128,1024]{2,1,0:T(8,128)} %param.10) | copy-start | bytes 1572868
  75.7 31.4 %copy-start.2 = (f32[1,128,1024]{2,1,0:T(8,128)S(1)}, f32[1,128,1024]{2,1,0:T(8,128)}, u32[]{:S(2)}) copy-start(f32[1,128,1024]{2,1,0:T(8,128)} %param.11) | copy-start | bytes 1572868
  75.7 70.4 %all-gather.3.cloned.1.call-start = ((), (), s32[]{:S(2)}) async-start(), calls=%async_computation.4 | async-start | bytes 4718592 | tf_op jit(solution)/shard_map/all_gather | solution.py:44
Sparse Core Ops, SparseCore 0:
  11.4 57.0 reduce-scatter.2
  75.8 31.1 reduce-scatter.4
  109.5 36.5 all-gather.2
where the time goes:
time: 166 us
  waiting for transfers between devices  125 us (75%)
  between operations  13.7 us (8%)
  other arithmetic  13.3 us (8%)
  local copies, waits for them, and re-layouts  12.9 us (8%)
    reduce_scatter x1, waiting for transfers between devices, local(): lax.psum_scatter(grad_parts[0, 0].astype(jnp.float32), 'fsdp', scatter_di...  57.2 us
    all_gather x1, waiting for transfers between devices, local(): lax.all_gather(params_new[None], ('replica', 'fsdp'), axis=0, tiled=True)  36.9 us
    reduce_scatter x1, waiting for transfers between devices, local(): lax.psum_scatter(updated, 'replica', scatter_dimension=1, tiled=True)  31.3 us
    broadcast_in_dim x1, other arithmetic, local(): second_out[None]  7.13 us
    transpose x1, local copies, waits for them, and re-layouts, local(): pieces.reshape(replicas, fsdp_count, row_count, share_cols)  6.86 us
    reshape x1, local copies, waits for them, and re-layouts, local(): arranged.reshape(row_count, fsdp_count * replicas * share_cols)  6.05 us
    convert_element_type x1, other arithmetic, local(): grad_parts[0, 0].astype(jnp.float32)  4.03 us
  transfers between devices with their start and end apart: 3, of which 3 were waited for; matrix products, arithmetic and copies ran while one was open for 0% of the time, Pallas kernels for 0%

commit v1 on v0

--- a/solution.py
+++ b/solution.py
@@ -11,6 +11,24 @@
 epsilon = 1e-08
 outer_rate = 0.7
 momentum_factor = 0.9
+
+
+def collect(value, axis, dim):
+    ways, here, hop = (lax.axis_size(axis), lax.axis_index(axis), value.shape[dim])
+    shape = [n * ways if d == dim else n for d, n in enumerate(value.shape)]
+    full = lax.dynamic_update_slice_in_dim(
+        jnp.zeros(shape, value.dtype), value, here * hop, axis=dim
+    )
+    going_up = going_down = value
+    for far in range(1, ways // 2 + 1):
+        going_up = lax.ppermute(going_up, axis, [(d, (d + 1) % ways) for d in range(ways)])
+        full = lax.dynamic_update_slice_in_dim(full, going_up, (here - far) % ways * hop, axis=dim)
+        if 2 * far < ways:
+            going_down = lax.ppermute(going_down, axis, [(d, (d - 1) % ways) for d in range(ways)])
+            full = lax.dynamic_update_slice_in_dim(
+                full, going_down, (here + far) % ways * hop, axis=dim
+            )
+    return full
 
 
 def inner_adamw(gradient, params, first_in, second_in):
@@ -41,7 +59,7 @@
     share_cols = outer_params.shape[2]
     totals = lax.psum_scatter(updated, "replica", scatter_dimension=1, tiled=True)
     params_new, momentum_new = nesterov(totals / replicas, outer_params[0], outer_momentum[0])
-    pieces = lax.all_gather(params_new[None], ("replica", "fsdp"), axis=0, tiled=True)
+    pieces = collect(params_new[None], ("replica", "fsdp"), 0)
     fsdp_count = lax.axis_size("fsdp")
     row_count = params_new.shape[0]
     arranged = pieces.reshape(replicas, fsdp_count, row_count, share_cols).transpose(2, 1, 0, 3)

time: 166 us -> 211 us (1.27)
  waiting for transfers between devices: 125 us -> 153 us
  starting transfers between devices: 0.12 us -> 10.8 us
  local copies, waits for them, and re-layouts: 12.9 us -> 20.4 us
    ppermute x0 -> x7, waiting for transfers between devices: none -> 64 us  [the longest x4 41.7 us: collect(): lax.ppermute(going_up, axis, [(d, (d + 1) % ways) for d in range(ways)])]
    all_gather x1 -> x0, waiting for transfers between devices: 36.9 us -> none  [local(): lax.all_gather(params_new[None], ('replica', 'fsdp'), axis=0, tiled=True)]
    ppermute x0 -> x7, starting transfers between devices: none -> 10.7 us  [the longest x3 5.88 us: collect(): lax.ppermute(going_down, axis, [(d, (d - 1) % ways) for d in range(ways)])]
    dynamic_update_slice x0 -> x7, local copies, waits for them, and re-layouts: none -> 6.87 us  [the longest x4 4.39 us: collect(): lax.dynamic_update_slice_in_dim(full, going_up, (here - far) % ways * hop...]
    reshape x1 -> x0, local copies, waits for them, and re-layouts: 6.05 us -> none  [local(): arranged.reshape(row_count, fsdp_count * replicas * share_cols)]
    unnamed x6 -> x15, local copies, waits for them, and re-layouts: 0.01 us -> 5.62 us
    broadcast_in_dim x0 -> x1, local copies, waits for them, and re-layouts: none -> 2.54 us  [collect(): jnp.zeros(shape, value.dtype)]
  transfers between devices with their start and end apart: 3 -> 9, of which waited for: 3 -> 9; matrix products, arithmetic and copies ran while one was open for 0% -> 3% of each run, Pallas kernels for 0% -> 0%
where the time goes in v1:
time: 211 us
  waiting for transfers between devices  153 us (73%)
  local copies, waits for them, and re-layouts  20.4 us (10%)
  between operations  14.1 us (7%)
  other arithmetic  13 us (6%)
  starting transfers between devices  10.8 us (5%)
    reduce_scatter x1, waiting for transfers between devices, local(): lax.psum_scatter(grad_parts[0, 0].astype(jnp.float32), 'fsdp', scatter_di...  57.2 us
    ppermute x4, waiting for transfers between devices, collect(): lax.ppermute(going_up, axis, [(d, (d + 1) % ways) for d in range(ways)])  41.7 us
    reduce_scatter x1, waiting for transfers between devices, local(): lax.psum_scatter(updated, 'replica', scatter_dimension=1, tiled=True)  31.3 us
    ppermute x3, waiting for transfers between devices, collect(): lax.ppermute(going_down, axis, [(d, (d - 1) % ways) for d in range(ways)])  22.2 us
    broadcast_in_dim x1, other arithmetic, local(): second_out[None]  7.13 us
    ppermute x3, starting transfers between devices, collect(): lax.ppermute(going_down, axis, [(d, (d - 1) % ways) for d in range(ways)])  5.88 us
    unnamed x15, local copies, waits for them, and re-layouts  5.62 us
    transpose x1, local copies, waits for them, and re-layouts, local(): pieces.reshape(replicas, fsdp_count, row_count, share_cols)  5.33 us
  transfers between devices with their start and end apart: 9, of which 9 were waited for; matrix products, arithmetic and copies ran while one was open for 3% of the time, Pallas kernels for 0%

profile of v1, /device:TPU:0, one launch (start us, length us, event | category | flops | bytes accessed | tf_op | source)
XLA Modules:
  0.0 210.8 jit_solution(9360150527827884832)
XLA Ops:
  7.2 0.0 reduce-scatter.3.cloned.1.call-start
  7.2 4.0 %bitcast_convert_fusion = f32[128,8192]{1,0:T(8,128)} fusion(bf16[1,1,128,8192]{3,2,1,0:T(8,128)(2,1)} %param.6), kind=kLoop, calls=%fused_computation.2 | loop fusion | flops 1048576 | bytes 6291456 | tf_op jit(solution)/shard_map/convert_element_type | solution.py:54
  11.3 0.0 reduce-scatter.5.cloned.1.call-start
  11.3 57.2 %reduce-scatter.3.cloned.1.call-done = f32[128,4096]{1,0:T(8,128)} async-done(((f32[128,8192]{1,0:T(8,128)}), f32[128,4096]{1,0:T(8,128)}) %reduce-scatter.3.cloned.1.call-update) | async-done | bytes 2097168 | tf_op jit(solution)/shard_map/reduce_scatter | solution.py:53
  68.5 7.1 %fusion.4 = (f32[1,128,4096]{2,1,0:T(8,128)}, f32[128,4096]{1,0:T(8,128)}, f32[1,128,4096]{2,1,0:T(8,128)}) fusion(f32[128,4096]{1,0:T(8,128)} %reduce-scatter.3.cloned.1.call-done, f32[1,128,4096]{2,1,0:T(8,128)S(1)} %copy-done, f32[1,128,4096]{2,1,0:T(8,128)} %param.8, f32[1,128,4096]{2,1,0:T(8,128)} %param.7), kind=kLoop, calls=%fused_computation.9 | loop fusion | flops 7864320 | bytes 14680064 | tf_op jit(solution)/shard_map/broadcast_in_dim | solution.py:67
  75.7 31.3 %reduce-scatter.5.cloned.1.call-done = f32[128,1024]{1,0:T(8,128)} async-done(((f32[128,4096]{1,0:T(8,128)}), f32[128,1024]{1,0:T(8,128)}) %reduce-scatter.5.cloned.1.call-update) | async-done | bytes 524304 | tf_op jit(solution)/shard_map/reduce_scatter | solution.py:60
  107.0 2.5 %broadcast_in_dim.16 = f32[8,128,1024]{2,1,0:T(8,128)} broadcast(f32[]{:T(128)} %constant.63.clone.1), dimensions={} | broadcast | bytes 4194308 | tf_op jit(solution)/shard_map/broadcast_in_dim | solution.py:20
  109.6 1.0 constant_dynamic-update-slice_fusion.7
  110.6 1.5 collective-permute-start
  112.0 1.2 collective-permute-start.1
  113.2 12.5 %collective-permute-done = f32[1,128,1024]{2,1,0:T(8,128)S(1)} collective-permute-done((f32[1,128,1024]{2,1,0:T(8,128)S(1)}, f32[1,128,1024]{2,1,0:T(8,128)S(1)}, u32[]{:S(2)}, u32[]{:S(2)}) %collective-permute-start) | collective-permute-done | bytes 524320 | tf_op jit(solution)/shard_map/ppermute | solution.py:24
  125.7 1.1 collective-permute-start.2
  126.8 9.2 %collective-permute-done.1 = f32[1,128,1024]{2,1,0:T(8,128)S(1)} collective-permute-done((f32[1,128,1024]{2,1,0:T(8,128)S(1)}, f32[1,128,1024]{2,1,0:T(8,128)S(1)}, u32[]{:S(2)}, u32[]{:S(2)}) %collective-permute-start.1) | collective-permute-done | bytes 524320 | tf_op jit(solution)/shard_map/ppermute | solution.py:27
  136.0 2.3 %collective-permute-start.3 = (f32[1,128,1024]{2,1,0:T(8,128)S(1)}, f32[1,128,1024]{2,1,0:T(8,128)S(1)}, u32[]{:S(2)}, u32[]{:S(2)}) collective-permute-start(f32[1,128,1024]{2,1,0:T(8,128)S(1)} %collective-permute-done.1), channel_id=1, source_target_pairs={{0,28},{4,0},{8,4},{12,8},{16,12},{20,16},{24,20},{28,24},{1,29},{... | collective-permute-start | bytes 1572872 | tf_op jit(solution)/shard_map/ppermute | solution.py:27
  138.4 9.9 %collective-permute-done.2 = f32[1,128,1024]{2,1,0:T(8,128)} collective-permute-done((f32[1,128,1024]{2,1,0:T(8,128)S(1)}, f32[1,128,1024]{2,1,0:T(8,128)}, u32[]{:S(2)}, u32[]{:S(2)}) %collective-permute-start.2) | collective-permute-done | bytes 524320 | tf_op jit(solution)/shard_map/ppermute | solution.py:24
  148.3 1.1 collective-permute-start.4
  149.4 0.9 fusion.6
  150.3 8.2 %collective-permute-done.3 = f32[1,128,1024]{2,1,0:T(8,128)S(1)} collective-permute-done((f32[1,128,1024]{2,1,0:T(8,128)S(1)}, f32[1,128,1024]{2,1,0:T(8,128)S(1)}, u32[]{:S(2)}, u32[]{:S(2)}) %collective-permute-start.3) | collective-permute-done | bytes 524320 | tf_op jit(solution)/shard_map/ppermute | solution.py:27
  158.5 2.3 %collective-permute-start.5 = (f32[1,128,1024]{2,1,0:T(8,128)S(1)}, f32[1,128,1024]{2,1,0:T(8,128)S(1)}, u32[]{:S(2)}, u32[]{:S(2)}) collective-permute-start(f32[1,128,1024]{2,1,0:T(8,128)S(1)} %collective-permute-done.3), channel_id=1, source_target_pairs={{0,28},{4,0},{8,4},{12,8},{16,12},{20,16},{24,20},{28,24},{1,29},{... | collective-permute-start | bytes 1572872 | tf_op jit(solution)/shard_map/ppermute | solution.py:27
  160.9 0.8 constant_dynamic-update-slice_fusion.6
  161.7 8.9 %collective-permute-done.4 = f32[1,128,1024]{2,1,0:T(8,128)S(1)} collective-permute-done((f32[1,128,1024]{2,1,0:T(8,128)}, f32[1,128,1024]{2,1,0:T(8,128)S(1)}, u32[]{:S(2)}, u32[]{:S(2)}) %collective-permute-start.4) | collective-permute-done | bytes 524320 | tf_op jit(solution)/shard_map/ppermute | solution.py:24
  170.6 1.1 collective-permute-start.6
  171.8 0.8 constant_dynamic-update-slice_fusion.5
  172.6 1.9 constant_dynamic-update-slice_fusion.4
  174.5 0.8 constant_dynamic-update-slice_fusion.3
  175.3 0.8 constant_dynamic-update-slice_fusion.2
  176.1 4.8 %collective-permute-done.5 = f32[1,128,1024]{2,1,0:T(8,128)S(1)} collective-permute-done((f32[1,128,1024]{2,1,0:T(8,128)S(1)}, f32[1,128,1024]{2,1,0:T(8,128)S(1)}, u32[]{:S(2)}, u32[]{:S(2)}) %collective-permute-start.5) | collective-permute-done | bytes 524320 | tf_op jit(solution)/shard_map/ppermute | solution.py:27
  181.0 0.8 constant_dynamic-update-slice_fusion.1
  181.8 10.4 %collective-permute-done.6 = f32[1,128,1024]{2,1,0:T(8,128)S(1)} collective-permute-done((f32[1,128,1024]{2,1,0:T(8,128)S(1)}, f32[1,128,1024]{2,1,0:T(8,128)S(1)}, u32[]{:S(2)}, u32[]{:S(2)}) %collective-permute-start.6) | collective-permute-done | bytes 524320 | tf_op jit(solution)/shard_map/ppermute | solution.py:24
  192.2 0.8 constant_dynamic-update-slice_fusion
  193.0 5.3 %copy.11 = f32[128,2,4,1024]{0,3,2,1:T(8,128)} copy(f32[128,2,4,1024]{3,0,1,2:T(8,128)} %bitcast.8) | data formatting | bytes 8388608 | tf_op jit(solution)/shard_map/transpose | solution.py:65
  198.4 5.6 %copy.12 = f32[128,8192]{1,0:T(8,128)} copy(f32[128,8192]{0,1:T(8,128)} %bitcast.58) | data formatting | bytes 8388608
  (16 shorter events, 0.1 us)
Async XLA Ops:
  7.2 61.4 %reduce-scatter.3.cloned.1.call-start = ((), (), s32[]{:S(2)}) async-start(), calls=%async_computation.2 | async-start | bytes 6291456 | tf_op jit(solution)/shard_map/reduce_scatter | solution.py:53
  11.2 57.3 %copy-start = (f32[1,128,4096]{2,1,0:T(8,128)S(1)}, f32[1,128,4096]{2,1,0:T(8,128)}, u32[]{:S(2)}) copy-start(f32[1,128,4096]{2,1,0:T(8,128)} %param.9) | copy-start | bytes 6291460
  11.3 95.8 %reduce-scatter.5.cloned.1.call-start = ((), (), s32[]{:S(2)}) async-start(), calls=%async_computation.3 | async-start | bytes 2621440 | tf_op jit(solution)/shard_map/reduce_scatter | solution.py:60
  75.7 33.9 %copy-start.1 = (f32[1,128,1024]{2,1,0:T(8,128)S(1)}, f32[1,128,1024]{2,1,0:T(8,128)}, u32[]{:S(2)}) copy-start(f32[1,128,1024]{2,1,0:T(8,128)} %param.11) | copy-start | bytes 1572868
  75.7 33.9 %copy-start.2 = (f32[1,128,1024]{2,1,0:T(8,128)S(1)}, f32[1,128,1024]{2,1,0:T(8,128)}, u32[]{:S(2)}) copy-start(f32[1,128,1024]{2,1,0:T(8,128)} %param.10) | copy-start | bytes 1572868
  107.0 2.5 %copy-start.3 = (f32[128,1024]{1,0:T(8,128)S(1)}, f32[128,1024]{1,0:T(8,128)}, u32[]{:S(2)}) copy-start(f32[128,1024]{1,0:T(8,128)} %reduce-scatter.5.cloned.1.call-done) | copy-start | bytes 1572868
  110.6 37.7 %copy-start.6 = (f32[1,128,1024]{2,1,0:T(8,128)}, f32[1,128,1024]{2,1,0:T(8,128)S(1)}, u32[]{:S(2)}) copy-start(f32[1,128,1024]{2,1,0:T(8,128)S(1)} %get-tuple-element.11) | copy-start | bytes 1572868
  110.6 15.1 %collective-permute-start = (f32[1,128,1024]{2,1,0:T(8,128)S(1)}, f32[1,128,1024]{2,1,0:T(8,128)S(1)}, u32[]{:S(2)}, u32[]{:S(2)}) collective-permute-start(f32[1,128,1024]{2,1,0:T(8,128)S(1)} %get-tuple-element.11), channel_id=1, source_target_pairs={{0,4},{4,8},{8,12},{12,16},{16,20},{20,24},{24,28},{28,0},{1,5},{5... | collective-permute-start | bytes 1572872 | tf_op jit(solution)/shard_map/ppermute | solution.py:24
  112.0 24.0 %collective-permute-start.1 = (f32[1,128,1024]{2,1,0:T(8,128)S(1)}, f32[1,128,1024]{2,1,0:T(8,128)S(1)}, u32[]{:S(2)}, u32[]{:S(2)}) collective-permute-start(f32[1,128,1024]{2,1,0:T(8,128)S(1)} %get-tuple-element.11), channel_id=1, source_target_pairs={{0,28},{4,0},{8,4},{12,8},{16,12},{20,16},{24,20},{28,24},{1,29},{... | collective-permute-start | bytes 1572872 | tf_op jit(solution)/shard_map/ppermute | solution.py:27
  125.7 12.7 %copy-start.4 = (f32[1,128,1024]{2,1,0:T(8,128)}, f32[1,128,1024]{2,1,0:T(8,128)S(1)}, u32[]{:S(2)}) copy-start(f32[1,128,1024]{2,1,0:T(8,128)S(1)} %collective-permute-done) | copy-start | bytes 1572868
  125.7 22.6 %collective-permute-start.2 = (f32[1,128,1024]{2,1,0:T(8,128)S(1)}, f32[1,128,1024]{2,1,0:T(8,128)}, u32[]{:S(2)}, u32[]{:S(2)}) collective-permute-start(f32[1,128,1024]{2,1,0:T(8,128)S(1)} %collective-permute-done), channel_id=1, source_target_pairs={{0,4},{4,8},{8,12},{12,16},{16,20},{20,24},{24,28},{28,0},{1,5},{5... | collective-permute-start | bytes 1572872 | tf_op jit(solution)/shard_map/ppermute | solution.py:24
  136.0 22.5 %collective-permute-start.3 = (f32[1,128,1024]{2,1,0:T(8,128)S(1)}, f32[1,128,1024]{2,1,0:T(8,128)S(1)}, u32[]{:S(2)}, u32[]{:S(2)}) collective-permute-start(f32[1,128,1024]{2,1,0:T(8,128)S(1)} %collective-permute-done.1), channel_id=1, source_target_pairs={{0,28},{4,0},{8,4},{12,8},{16,12},{20,16},{24,20},{28,24},{1,29},{... | collective-permute-start | bytes 1572872 | tf_op jit(solution)/shard_map/ppermute | solution.py:27
  148.3 22.4 %collective-permute-start.4 = (f32[1,128,1024]{2,1,0:T(8,128)}, f32[1,128,1024]{2,1,0:T(8,128)S(1)}, u32[]{:S(2)}, u32[]{:S(2)}) collective-permute-start(f32[1,128,1024]{2,1,0:T(8,128)} %collective-permute-done.2), channel_id=1, source_target_pairs={{0,4},{4,8},{8,12},{12,16},{16,20},{20,24},{24,28},{28,0},{1,5},{5... | collective-permute-start | bytes 1572872 | tf_op jit(solution)/shard_map/ppermute | solution.py:24
  149.4 11.5 %copy-start.5 = (f32[1,128,1024]{2,1,0:T(8,128)S(1)}, f32[1,128,1024]{2,1,0:T(8,128)}, u32[]{:S(2)}) copy-start(f32[1,128,1024]{2,1,0:T(8,128)} %copy-done.4) | copy-start | bytes 1572868
  158.5 22.5 %collective-permute-start.5 = (f32[1,128,1024]{2,1,0:T(8,128)S(1)}, f32[1,128,1024]{2,1,0:T(8,128)S(1)}, u32[]{:S(2)}, u32[]{:S(2)}) collective-permute-start(f32[1,128,1024]{2,1,0:T(8,128)S(1)} %collective-permute-done.3), channel_id=1, source_target_pairs={{0,28},{4,0},{8,4},{12,8},{16,12},{20,16},{24,20},{28,24},{1,29},{... | collective-permute-start | bytes 1572872 | tf_op jit(solution)/shard_map/ppermute | solution.py:27
  170.6 21.6 %collective-permute-start.6 = (f32[1,128,1024]{2,1,0:T(8,128)S(1)}, f32[1,128,1024]{2,1,0:T(8,128)S(1)}, u32[]{:S(2)}, u32[]{:S(2)}) collective-permute-start(f32[1,128,1024]{2,1,0:T(8,128)S(1)} %collective-permute-done.4), channel_id=1, source_target_pairs={{0,4},{4,8},{8,12},{12,16},{16,20},{20,24},{24,28},{28,0},{1,5},{5... | collective-permute-start | bytes 1572872 | tf_op jit(solution)/shard_map/ppermute | solution.py:24
Sparse Core Ops, SparseCore 0:
  11.4 57.0 reduce-scatter.2
  75.8 31.1 reduce-scatter.4
